TPU v7x, 256 devices: a whole 4x4x8 slice. The times are simulated.
256 devices in a mesh: row: 8 (over y, x_lo), col: 32 (over x_hi, z, core).
Axes of the slice: x: 4 (x_hi: 2, x_lo: 2; x = x_hi * 2 + x_lo), y: 4, z: 8, core: 2. Of those that a mesh axis runs over, the one named last changes fastest.
Arguments:
- vectors: bfloat16 [16, 131072], P(None, ('row', 'col')), may hold values from -6 to 6
- blocks: bfloat16 [8, 6144, 128, 128], P('row', 'col'), may hold values from -0.09375 to 0.09375
- row_ptr: int32 [8, 4128], P('row', 'col'), may hold values from 0 to 192, as said below
- col_idx: int32 [8, 6144], P('row', 'col'), may hold values from 0 to 31, as said below
Outputs:
- product: float32 [16, 131072], P(None, ('row', 'col'))
Inputs may be any that keep to these rules, and one draw needn't show every extreme that they name: For each tile, row_ptr starts at 0, never falls, and ends at the tile's count of live slots; at least one tile has exactly 192 live slots in every draw, and counts differ strongly from tile to tile. `col_idx`: within each block row of a tile the live slots name strictly rising block columns, so no block position of a tile is stored twice; slots at or past a tile's count hold a valid column and are unused.
All inputs are finite; a program needn't handle non-finite values.
Results may differ from a plain program's by a relative error of at most 0.0003.
Values may be sent and summed in bfloat16 or wider, within the bound.
No kernel may reach another device: no remote copies, remote signals or barrier semaphores. Data moves between devices by JAX's collectives and lax.ppermute only.
A program may use at most 64 MiB of HBM per device.

v0:
```python
import jax
import jax.numpy as jnp
from jax import lax
from jax.sharding import PartitionSpec as P


def tile_terms(row_side, col_side, tile_blocks, pointers, columns):
    slot_ids = jnp.arange(tile_blocks.shape[0], dtype=jnp.int32)
    live_slots = slot_ids < pointers[-1]
    slot_rows = jnp.sum((slot_ids[:, None] >= pointers[None, 1:]).astype(jnp.int32), axis=1)
    slot_rows = jnp.minimum(slot_rows, pointers.shape[0] - 2)
    count_vectors = row_side.shape[0]
    edge = tile_blocks.shape[1]
    row_blocks = row_side.reshape(count_vectors, -1, edge)
    col_blocks = col_side.reshape(count_vectors, -1, edge)
    picked_rows = jnp.take(row_blocks, slot_rows, axis=1)
    picked_cols = jnp.take(col_blocks, columns, axis=1)
    forward = jnp.einsum(
        "ksj,sij->ski", picked_cols, tile_blocks, preferred_element_type=jnp.float32
    )
    backward = jnp.einsum(
        "ksi,sij->skj", picked_rows, tile_blocks, preferred_element_type=jnp.float32
    )
    live_mask = live_slots[:, None, None]
    forward = jnp.where(live_mask, forward, jnp.zeros_like(forward))
    backward = jnp.where(live_mask, backward, jnp.zeros_like(backward))
    forward_sum = jax.ops.segment_sum(
        forward, slot_rows, num_segments=row_blocks.shape[1], indices_are_sorted=True
    )
    backward_sum = jax.ops.segment_sum(backward, columns, num_segments=col_blocks.shape[1])
    return (forward_sum, backward_sum)


def body(vectors, blocks, row_ptr, col_idx):
    count_vectors = vectors.shape[0]
    segment = vectors.shape[1]
    grid_rows = lax.axis_size("row")
    grid_cols = lax.axis_size("col")
    everything = lax.all_gather(vectors, ("row", "col"), axis=1, tiled=True)
    row_side = lax.dynamic_slice_in_dim(
        everything, lax.axis_index("row") * (grid_cols * segment), grid_cols * segment, 1
    )
    spread = everything.reshape(count_vectors, grid_rows, grid_cols, segment)
    col_side = lax.dynamic_slice_in_dim(spread, lax.axis_index("col"), 1, 2).reshape(
        count_vectors, grid_rows * segment
    )
    forward_sum, backward_sum = tile_terms(row_side, col_side, blocks[0], row_ptr[0], col_idx[0])
    forward_part = lax.psum_scatter(forward_sum, "col", scatter_dimension=0, tiled=True)
    backward_part = lax.psum_scatter(backward_sum, "row", scatter_dimension=0, tiled=True)
    combined = forward_part + backward_part
    return combined.transpose(1, 0, 2).reshape(count_vectors, segment)


def solution(mesh):
    in_specs = (
        P(None, ("row", "col")),
        P("row", "col", None, None),
        P("row", "col"),
        P("row", "col"),
    )
    out_specs = P(None, ("row", "col"))
    return jax.shard_map(body, mesh=mesh, in_specs=in_specs, out_specs=out_specs, check_vma=False)
```

profile of v0, /device:TPU:8, one launch (start us, length us, event | category | flops | bytes accessed | tf_op | source)
XLA Modules:
  0.0 608.5 jit_solution(9309983485756426636)
XLA Ops:
  6.5 0.7 all-gather.2.cloned.1.call-update
  7.3 0.0 reduce-scatter.5.cloned.1.call-start
  7.3 1.2 slice.9
  8.5 0.6 iota_compare_fusion.1
  9.1 0.8 slice_bitcast_fusion
  9.9 0.1 convert_reduce_fusion
  10.1 0.7 compare_and_fusion.1
  10.7 0.7 compare_select_fusion.1
  11.4 413.9 %all-gather.2.cloned.1.call-done = bf16[16,131072]{1,0:T(8,128)(2,1)} async-done(((bf16[16,512]{1,0:T(8,128)(2,1)}), bf16[16,131072]{1,0:T(8,128)(2,1)}) %all-gather.2.cloned.1.call-update) | async-done | bytes 4194320 | tf_op jit(solution)/shard_map/all_gather | solution.py:39
  425.3 1.1 copy_bitcast_fusion
  426.4 0.8 gather_fusion.1
  427.2 0.0 copy-start.2
  427.2 4.2 fusion.7
  431.5 0.0 copy-done.2
  431.5 7.6 %scatter_fusion.1 = f32[32,16,128]{2,1,0:T(8,128)S(1)} fusion(f32[32,16,128]{2,1,0:T(8,128)S(1)} %broadcast_in_dim.43, s32[192]{0:T(256)S(1)} %bitcast.42, f32[192,16,128]{2,1,0:T(8,128)S(1)} %fusion.7), kind=kCustom, calls=%fused_computation.3 | custom fusion | flops 393216 | bytes 4719360 | tf_op jit(solution)/shard_map/scatter-add | solution.py:30
  439.1 0.7 copy-done
  439.8 0.0 reduce-scatter.5.cloned.1.call-update
  439.8 0.0 reduce-scatter.3.cloned.1.call-start
  439.9 3.6 copy.18
  443.5 0.8 dynamic-slice_reduce_fusion
  444.3 0.1 reshape_reshape.3
  444.4 0.1 copy.12
  444.4 0.8 gather_fusion
  445.2 5.8 fusion.4
  451.0 0.1 broadcast_in_dim.39
  451.1 7.9 %scatter_fusion = f32[128,16,128]{2,1,0:T(8,128)S(1)} fusion(f32[128,16,128]{2,1,0:T(8,128)S(1)} %broadcast_in_dim.39, s32[192]{0:T(256)S(1)} %broadcast_minimum_fusion, f32[192,16,128]{2,1,0:T(8,128)S(1)} %fusion.4), kind=kCustom, calls=%fused_computation.2 | custom fusion | flops 393216 | bytes 4719360 | tf_op jit(solution)/shard_map/scatter-add | solution.py:27
  459.1 0.0 copy-start.1
  459.1 1.0 copy-done.1
  460.1 0.0 reduce-scatter.3.cloned.1.call-update
  460.1 19.7 %reduce-scatter.5.cloned.1.call-done = f32[4,16,128]{2,1,0:T(8,128)} async-done(((f32[32,16,128]{2,1,0:T(8,128)}), f32[4,16,128]{2,1,0:T(8,128)}) %reduce-scatter.5.cloned.1.call-update) | async-done | bytes 32784 | tf_op jit(solution)/shard_map/reduce_scatter | solution.py:49
  479.8 120.8 %reduce-scatter.3.cloned.1.call-done = f32[4,16,128]{2,1,0:T(8,128)} async-done(((f32[128,16,128]{2,1,0:T(8,128)}), f32[4,16,128]{2,1,0:T(8,128)}) %reduce-scatter.3.cloned.1.call-update) | async-done | bytes 32784 | tf_op jit(solution)/shard_map/reduce_scatter | solution.py:48
  600.6 1.4 copy_bitcast_fusion.1
  (8 shorter events, 0.1 us)
Async XLA Ops:
  6.5 418.8 %all-gather.2.cloned.1.call-start = ((), (), s32[]{:S(2)}) async-start(), calls=%async_computation.2 | async-start | bytes 4210688 | tf_op jit(solution)/shard_map/all_gather | solution.py:39
  7.3 472.5 %reduce-scatter.5.cloned.1.call-start = ((), (), s32[]{:S(2)}) async-start(), calls=%async_computation.4 | async-start | bytes 294912 | tf_op jit(solution)/shard_map/reduce_scatter | solution.py:49
  427.2 4.3 copy-start.2
  439.1 0.7 copy-start
  439.8 160.8 %reduce-scatter.3.cloned.1.call-start = ((), (), s32[]{:S(2)}) async-start(), calls=%async_computation.3 | async-start | bytes 1081344 | tf_op jit(solution)/shard_map/reduce_scatter | solution.py:48
  459.1 1.0 copy-start.1
Sparse Core Ops, SparseCore 0:
  9.2 416.0 all-gather.1
  439.9 39.8 reduce-scatter.4
  483.9 116.6 reduce-scatter.2
where the time goes:
time: 609 us
  waiting for transfers between devices  555 us (91%)
  other arithmetic  19.1 us (3%)
  between operations  13.3 us (2%)
  local copies, waits for them, and re-layouts  10.9 us (2%)
  matrix products  10.1 us (2%)
    all_gather x1, waiting for transfers between devices, body(): everything = lax.all_gather(vectors, ('row', 'col'), axis=1, tiled=True)  414 us
    reduce_scatter x1, waiting for transfers between devices, body(): lax.psum_scatter(forward_sum, 'col', scatter_dimension=0, tiled=True)  121 us
    reduce_scatter x1, waiting for transfers between devices, body(): lax.psum_scatter(backward_sum, 'row', scatter_dimension=0, tiled=True)  19.7 us
  transfers between devices with their start and end apart: 3, of which 3 were waited for; matrix products, arithmetic and copies ran while one was open for 4% of the time, Pallas kernels for 0%

commit v1 on v0

--- a/solution.py
+++ b/solution.py
@@ -36,7 +36,14 @@
     segment = vectors.shape[1]
     grid_rows = lax.axis_size("row")
     grid_cols = lax.axis_size("col")
-    everything = lax.all_gather(vectors, ("row", "col"), axis=1, tiled=True)
+
+    def _order_entries(values):
+        kept_arr = jnp.stack([values for _ in range(lax.axis_size(("row", "col")))], 0)
+        next_value = lax.all_to_all(kept_arr, ("row", "col"), 0, 0)
+        mixed_arr = jnp.concatenate(next_value, 1)
+        return mixed_arr
+
+    everything = _order_entries(vectors)
     row_side = lax.dynamic_slice_in_dim(
         everything, lax.axis_index("row") * (grid_cols * segment), grid_cols * segment, 1
     )

time: 609 us -> 301 us (0.49)
  waiting for transfers between devices: 555 us -> 233 us
  starting transfers between devices: 0.08 us -> 15.7 us
    all_gather x1 -> x0, waiting for transfers between devices: 414 us -> none  [body(): everything = lax.all_gather(vectors, ('row', 'col'), axis=1, tiled=True)]
    all_to_all x0 -> x1, waiting for transfers between devices: none -> 92.5 us  [_order_entries(): next_value = lax.all_to_all(kept_arr, ('row', 'col'), 0, 0)]
    all_to_all x0 -> x1, starting transfers between devices: none -> 15.6 us  [_order_entries(): next_value = lax.all_to_all(kept_arr, ('row', 'col'), 0, 0)]
  transfers between devices with their start and end apart: 3 -> 3, of which waited for: 3 -> 3; matrix products, arithmetic and copies ran while one was open for 4% -> 6% of each run, Pallas kernels for 0% -> 0%
where the time goes in v1:
time: 301 us
  waiting for transfers between devices  233 us (77%)
  other arithmetic  17.7 us (6%)
  starting transfers between devices  15.7 us (5%)
  between operations  13.6 us (5%)
  local copies, waits for them, and re-layouts  10.9 us (4%)
  matrix products  10.1 us (3%)
    reduce_scatter x1, waiting for transfers between devices, body(): lax.psum_scatter(forward_sum, 'col', scatter_dimension=0, tiled=True)  121 us
    all_to_all x1, waiting for transfers between devices, _order_entries(): next_value = lax.all_to_all(kept_arr, ('row', 'col'), 0, 0)  92.5 us
    reduce_scatter x1, waiting for transfers between devices, body(): lax.psum_scatter(backward_sum, 'row', scatter_dimension=0, tiled=True)  19.3 us
    all_to_all x1, starting transfers between devices, _order_entries(): next_value = lax.all_to_all(kept_arr, ('row', 'col'), 0, 0)  15.6 us
    scatter-add x1, other arithmetic, tile_terms(): jax.ops.segment_sum(forward, slot_rows, num_segments=row_blocks.shape[1],...  7.95 us
    scatter-add x1, other arithmetic, tile_terms(): jax.ops.segment_sum(backward, columns, num_segments=col_blocks.shape[1])  7.57 us
  transfers between devices with their start and end apart: 3, of which 3 were waited for; matrix products, arithmetic and copies ran while one was open for 6% of the time, Pallas kernels for 0%

profile of v1, /device:TPU:8, one launch (start us, length us, event | category | flops | bytes accessed | tf_op | source)
XLA Modules:
  0.0 300.6 jit_solution(6476918184411494468)
XLA Ops:
  6.5 3.2 %stack.2 = bf16[256,16,512]{2,1,0:T(8,128)(2,1)} broadcast(bf16[16,512]{1,0:T(8,128)(2,1)} %param.4), dimensions={1,2} | broadcast | bytes 4210688 | tf_op jit(solution)/shard_map/stack | solution.py:41
  9.8 15.6 %all-to-all-start = ((bf16[256,16,512]{2,1,0:T(8,128)(2,1)}), bf16[256,16,512]{2,1,0:T(8,128)(2,1)}, u32[]{:S(2)}, u32[]{:S(2)}) async-start(bf16[256,16,512]{2,1,0:T(8,128)(2,1)} %stack.2), calls=%async_computation | async-start | bytes 8388608 | tf_op jit(solution)/shard_map/all_to_all | solution.py:42
  25.4 0.0 reduce-scatter.5.cloned.1.call-start
  25.4 0.0 copy-done.3
  25.4 0.5 slice.9
  25.9 0.6 iota_compare_fusion.1
  26.6 0.1 slice_bitcast_fusion
  26.7 0.1 convert_reduce_fusion
  26.8 0.0 copy-done.2
  26.9 92.5 %all-to-all-done = bf16[256,16,512]{2,1,0:T(8,128)(2,1)} async-done(((bf16[256,16,512]{2,1,0:T(8,128)(2,1)}), bf16[256,16,512]{2,1,0:T(8,128)(2,1)}, u32[]{:S(2)}, u32[]{:S(2)}) %all-to-all-start) | async-done | bytes 4194336 | tf_op jit(solution)/shard_map/all_to_all | solution.py:42
  119.4 2.5 copy.23
  121.9 0.1 copy_bitcast_fusion
  122.0 0.8 gather_fusion.1
  122.8 4.2 %fusion.7 = f32[192,16,128]{2,1,0:T(8,128)S(1)} fusion(bf16[1,192,128,128]{3,2,1,0:T(8,128)(2,1)} %param.5, bf16[192,16,128]{2,1,0:T(8,128)(2,1)S(1)} %gather_fusion.1, pred[192]{0:T(512)(128)(4,1)S(1)} %compare_and_fusion, pred[192]{0:T(512)(128)(4,1)S(1)} %iota_compare_fusion.1), kind=kOutput, calls=%fused_computation.9 | convolution fusion | flops 101449728 | bytes 8651136 | tf_op jit(solution)/shard_map/ksi,sij->skj/dot_general | solution.py:21
  127.1 7.6 %scatter_fusion.1 = f32[32,16,128]{2,1,0:T(8,128)S(1)} fusion(f32[32,16,128]{2,1,0:T(8,128)S(1)} %broadcast_in_dim.43, s32[192]{0:T(256)S(1)} %bitcast.47, f32[192,16,128]{2,1,0:T(8,128)S(1)} %fusion.7), kind=kCustom, calls=%fused_computation.3 | custom fusion | flops 393216 | bytes 4719360 | tf_op jit(solution)/shard_map/scatter-add | solution.py:30
  134.7 0.7 copy-done
  135.3 0.0 reduce-scatter.5.cloned.1.call-update
  135.4 0.0 reduce-scatter.3.cloned.1.call-start
  135.4 0.9 constant_dynamic-slice_fusion
  136.3 0.1 copy.21
  136.4 0.1 reshape_reshape.7
  136.5 0.1 copy.17
  136.6 0.8 gather_fusion
  137.4 5.8 %fusion.4 = f32[192,16,128]{2,1,0:T(8,128)S(1)} fusion(bf16[1,192,128,128]{3,2,1,0:T(8,128)(2,1)} %param.5, bf16[192,16,128]{2,1,0:T(8,128)(2,1)S(1)} %gather_fusion, pred[192]{0:T(512)(128)(4,1)S(1)} %compare_and_fusion.1, pred[192]{0:T(512)(128)(4,1)S(1)} %iota_compare_fusion.1), kind=kOutput, calls=%fused_computation.8 | convolution fusion | flops 101449728 | bytes 8651136 | tf_op jit(solution)/shard_map/ksj,sij->ski/dot_general | solution.py:18
  143.2 0.1 broadcast_in_dim.39
  143.3 7.9 %scatter_fusion = f32[128,16,128]{2,1,0:T(8,128)S(1)} fusion(f32[128,16,128]{2,1,0:T(8,128)S(1)} %broadcast_in_dim.39, s32[192]{0:T(256)S(1)} %broadcast_minimum_fusion, f32[192,16,128]{2,1,0:T(8,128)S(1)} %fusion.4), kind=kCustom, calls=%fused_computation.2 | custom fusion | flops 393216 | bytes 4719360 | tf_op jit(solution)/shard_map/scatter-add | solution.py:27
  151.2 0.0 copy-start.1
  151.2 1.0 copy-done.1
  152.2 0.0 reduce-scatter.3.cloned.1.call-update
  152.2 19.3 %reduce-scatter.5.cloned.1.call-done = f32[4,16,128]{2,1,0:T(8,128)} async-done(((f32[32,16,128]{2,1,0:T(8,128)}), f32[4,16,128]{2,1,0:T(8,128)}) %reduce-scatter.5.cloned.1.call-update) | async-done | bytes 32784 | tf_op jit(solution)/shard_map/reduce_scatter | solution.py:56
  171.5 120.8 %reduce-scatter.3.cloned.1.call-done = f32[4,16,128]{2,1,0:T(8,128)} async-done(((f32[128,16,128]{2,1,0:T(8,128)}), f32[4,16,128]{2,1,0:T(8,128)}) %reduce-scatter.3.cloned.1.call-update) | async-done | bytes 32784 | tf_op jit(solution)/shard_map/reduce_scatter | solution.py:55
  292.3 1.4 copy_bitcast_fusion.1
  (11 shorter events, 0.1 us)
Async XLA Ops:
  9.8 15.7 %copy-start.3 = (s32[1,129]{1,0:T(1,128)S(1)}, s32[1,129]{1,0:T(1,128)}, u32[]{:S(2)}) copy-start(s32[1,129]{1,0:T(1,128)} %param.6) | copy-start | bytes 1552
  9.8 17.1 %copy-start.2 = (s32[1,192]{1,0:T(1,128)S(1)}, s32[1,192]{1,0:T(1,128)}, u32[]{:S(2)}) copy-start(s32[1,192]{1,0:T(1,128)} %param.7) | copy-start | bytes 2308
  9.8 109.6 %all-to-all-start = ((bf16[256,16,512]{2,1,0:T(8,128)(2,1)}), bf16[256,16,512]{2,1,0:T(8,128)(2,1)}, u32[]{:S(2)}, u32[]{:S(2)}) async-start(bf16[256,16,512]{2,1,0:T(8,128)(2,1)} %stack.2), calls=%async_computation | async-start | bytes 8388608 | tf_op jit(solution)/shard_map/all_to_all | solution.py:42
  25.4 146.1 %reduce-scatter.5.cloned.1.call-start = ((), (), s32[]{:S(2)}) async-start(), calls=%async_computation.4 | async-start | bytes 294912 | tf_op jit(solution)/shard_map/reduce_scatter | solution.py:56
  134.6 0.7 copy-start
  135.4 157.0 %reduce-scatter.3.cloned.1.call-start = ((), (), s32[]{:S(2)}) async-start(), calls=%async_computation.3 | async-start | bytes 1081344 | tf_op jit(solution)/shard_map/reduce_scatter | solution.py:55
  151.2 1.0 copy-start.1
Sparse Core Ops, SparseCore 0:
  135.5 35.9 reduce-scatter.4
  175.6 116.7 reduce-scatter.2
